TPU v7x, 32 devices: a whole 2x2x4 slice. The times are simulated.
32 devices in a mesh: groups: 2 (over x), wide: 4 (over y, core), expert: 4 (over z).
Axes of the slice: x: 2, y: 2, z: 4, core: 2. Of those that a mesh axis runs over, the one named last changes fastest.
Arguments:
- prompts: bfloat16 [8, 128, 6144], P(('groups', 'wide'), None, 'expert'), parts along dimension 0, may hold values from -6 to 6
- span_slot_owner: int32 [8], P('groups'), parts along dimension 0, may hold values from 0 to 3, as said below
- row_expert_index: int32 [768, 2], P('groups'), parts along dimension 0, may hold values from 0 to 7, all different within a row
- tile_tenant_index: int32 [6], P('groups'), parts along dimension 0, may hold values from 0 to 7
- tenant_adapter_slot: int32 [16], P('groups'), parts along dimension 0, may hold values from 0 to 7, each once
- router: bfloat16 [6144, 8], replicated, may hold values from -0.078125 to 0.078125
- gate_weight: bfloat16 [2, 6144, 16384], P(None, None, ('wide', 'expert')), may hold values from -0.078125 to 0.078125
- up_weight: bfloat16 [2, 6144, 16384], P(None, None, ('wide', 'expert')), may hold values from -0.078125 to 0.078125
- down_weight: bfloat16 [2, 16384, 6144], P(None, 'wide', 'expert'), may hold values from -0.046875 to 0.046875
- adapter_down_weight: bfloat16 [16, 2, 6144, 64], P(('groups', 'wide'), None, 'expert'), parts along dimension 0, may hold values from -0.078125 to 0.078125
- adapter_up_weight: bfloat16 [16, 2, 64, 16384], P('groups', None, None, ('wide', 'expert')), parts along dimension 0, may hold values from -0.75 to 0.75
Outputs:
- mixed: bfloat16 [768, 6144], P(('groups', 'wide'), 'expert'), parts along dimension 0
There are 2 independent parts, one for each index of `groups`. A program takes and returns all parts, laid end to end along the dimension named above; an argument that names none is the same for every part. Nothing has to cross between parts.
Inputs may be any that keep to these rules, and one draw needn't show every extreme that they name: `span_slot_owner`: a permutation of the slots; span c, for c < 3, is in slot span_slot_owner[c]. `row_expert_index`: each row names two different experts. `tenant_adapter_slot`: a permutation of the slots. `tile_tenant_index`: tenant of rows 128 * i to 128 * i + 127.
All inputs are finite; a program needn't handle non-finite values.
Results may differ from a plain program's by a relative error of at most 0.0051.
Values may be sent and summed in bfloat16 or wider, within the bound.
No kernel may reach another device: no remote copies, remote signals or barrier semaphores. Data moves between devices by JAX's collectives and lax.ppermute only.
A program may use at most 128 MiB of HBM per device.

v0:
```python
import jax
import jax.numpy as jnp
import numpy as np
from jax import lax
from jax.sharding import Mesh
from jax.sharding import PartitionSpec as P

ADAPTER_SCALE = 0.5
WIDE = ("wy", "wc")
GROUP = ("wy", "wc", "expert")


def per_device(
    prompts,
    span_slot_owner,
    row_expert_index,
    tile_tenant_index,
    tenant_adapter_slot,
    router,
    gate_weight,
    up_weight,
    down_weight,
    adapter_down_weight,
    adapter_up_weight,
):
    span = prompts.shape[1]
    quarter = prompts.shape[2]
    tokens = row_expert_index.shape[0]
    nchunk = tokens // span
    window = gate_weight.shape[0]
    core = lax.axis_index("wc")
    cores = lax.axis_size("wc")
    wide_index = lax.axis_index(WIDE)
    tile_count = tile_tenant_index.shape[0]
    tile_rows = tokens // tile_count
    resident_slots = adapter_down_weight.shape[0]
    rank = adapter_down_weight.shape[3]
    slot_of_span = span_slot_owner[:nchunk]
    held_slots = prompts.shape[0]
    if lax.axis_size("wy") == 2 and cores == 2:
        pair = [(0, 1), (1, 0)]
        slot_chip = lax.ppermute(prompts, "wy", pair)
        slot_core = lax.ppermute(prompts, "wc", pair)
        slot_both = lax.ppermute(slot_chip, "wc", pair)
        slots_q = jnp.concatenate([prompts, slot_core, slot_chip, slot_both], axis=0)
        slot_pick = (
            jnp.bitwise_xor(slot_of_span // held_slots, wide_index) * held_slots
            + slot_of_span % held_slots
        )
    else:
        slots_q = lax.all_gather(prompts, WIDE, axis=0, tiled=True)
        slot_pick = slot_of_span
    rows_q = jnp.take(slots_q, slot_pick, axis=0).reshape(tokens, quarter)
    chips = lax.axis_size("wy")
    tile_slot_index = jnp.take(tenant_adapter_slot, tile_tenant_index)
    holder = tile_slot_index // resident_slots
    local_slot = tile_slot_index % resident_slots
    if chips == 2 and cores == 2:
        swap = [(0, 1), (1, 0)]
        from_chip = lax.ppermute(adapter_down_weight, "wy", swap)
        from_core = lax.ppermute(adapter_down_weight, "wc", swap)
        from_both = lax.ppermute(from_chip, "wc", swap)
        stacked = jnp.stack([adapter_down_weight, from_core, from_chip, from_both])
        source = jnp.bitwise_xor(holder, wide_index)
    else:
        stacked = lax.all_gather(adapter_down_weight, WIDE, axis=0, tiled=False)
        source = holder
    flat_held = stacked.reshape((-1,) + adapter_down_weight.shape[1:])
    tile_adapters = jnp.take(flat_held, source * resident_slots + local_slot, axis=0)
    partial_rank = jnp.einsum(
        "ntd,nedr->nter",
        rows_q.reshape(tile_count, tile_rows, quarter),
        tile_adapters,
        preferred_element_type=jnp.float32,
    ).reshape(tokens, window * rank)
    rank_top = lax.reduce_precision(partial_rank, exponent_bits=8, mantissa_bits=7)
    rank_hi = rank_top.astype(jnp.bfloat16)
    rank_lo = (partial_rank - rank_top).astype(jnp.bfloat16)
    half = tokens // cores
    expert_size = lax.axis_size("expert")
    swap = [(i, (i + 1) % cores) for i in range(cores)]
    mine_q = lax.dynamic_slice_in_dim(rows_q, core * half, half, 0)
    mine = lax.all_gather(mine_q, "expert", axis=1, tiled=True)
    rank_q = lax.dynamic_slice_in_dim(
        jnp.concatenate([rank_hi, rank_lo], axis=1), core * half, half, 0
    )
    rank_q, _ = lax.optimization_barrier((rank_q, mine))
    pieces = lax.all_gather(rank_q, "expert", axis=1, tiled=False).astype(jnp.float32)
    mine_rank = jnp.sum(pieces[:, :, : window * rank] + pieces[:, :, window * rank :], axis=1)
    mine_rank = mine_rank.astype(jnp.bfloat16)
    other = lax.ppermute(mine, "wc", swap)
    other_rank = lax.ppermute(mine_rank, "wc", swap)
    input_rows = jnp.where(
        core == 0, jnp.concatenate([mine, other], axis=0), jnp.concatenate([other, mine], axis=0)
    )
    input_rows = lax.optimization_barrier(input_rows)
    lowrank = jnp.where(
        core == 0,
        jnp.concatenate([mine_rank, other_rank], axis=0),
        jnp.concatenate([other_rank, mine_rank], axis=0),
    ).reshape(tile_count, tile_rows, window, rank)
    logits = jnp.dot(input_rows, router, preferred_element_type=jnp.float32)
    experts = jnp.arange(router.shape[1], dtype=jnp.int32)
    picked = (row_expert_index[:, :, None] == experts[None, None, :]).astype(jnp.float32)
    chosen = jnp.sum(picked * logits[:, None, :], axis=2)
    first_prob = jax.nn.sigmoid(chosen[:, 0] - chosen[:, 1])
    second_prob = jax.nn.sigmoid(chosen[:, 1] - chosen[:, 0])
    weight = (
        first_prob[:, None] * picked[:, 0, :window] + second_prob[:, None] * picked[:, 1, :window]
    )
    tile_up = jnp.take(adapter_up_weight, tile_tenant_index, axis=0)
    adapted_hidden = jnp.einsum(
        "nter,nerf->ntef", lowrank, tile_up, preferred_element_type=jnp.float32
    ).reshape(tokens, window, tile_up.shape[3])
    running = None
    for expert_number in range(window):
        gate_pre = jnp.dot(
            input_rows, gate_weight[expert_number], preferred_element_type=jnp.float32
        )
        up_value = (
            jnp.dot(input_rows, up_weight[expert_number], preferred_element_type=jnp.float32)
            + ADAPTER_SCALE * adapted_hidden[:, expert_number]
        )
        hidden = (weight[:, expert_number, None] * jax.nn.silu(gate_pre) * up_value).astype(
            jnp.bfloat16
        )
        gathered = lax.all_gather(hidden, "expert", axis=1, tiled=True)
        part = jnp.dot(gathered, down_weight[expert_number], preferred_element_type=jnp.float32)
        running = part if running is None else running + part
    return reduce_rows(running, core, cores).astype(jnp.bfloat16)


def reduce_rows(running, core, cores):
    chips = lax.axis_size("wy")
    block = running.shape[0] // (chips * cores)
    by_chip = running.reshape(chips, cores, block, running.shape[1])
    keep = jnp.where(core == 0, by_chip[:, 0], by_chip[:, 1])
    send = jnp.where(core == 0, by_chip[:, 1], by_chip[:, 0])
    chip_sum = keep + lax.ppermute(send, "wc", [(i, (i + 1) % cores) for i in range(cores)])
    if chips == 2:
        chip = lax.axis_index("wy")
        mine = jnp.where(chip == 0, chip_sum[0], chip_sum[1])
        away = jnp.where(chip == 0, chip_sum[1], chip_sum[0])
        arrived = lax.ppermute(away.astype(jnp.bfloat16), "wy", [(0, 1), (1, 0)])
        return mine + arrived.astype(jnp.float32)
    return lax.psum_scatter(chip_sum, "wy", scatter_dimension=0, tiled=True).reshape(block, -1)


def solution(mesh):
    groups = mesh.shape["groups"]
    wide = mesh.shape["wide"]
    expert = mesh.shape["expert"]
    split = Mesh(
        np.asarray(mesh.devices).reshape(groups, wide // 2, 2, expert),
        ("groups", "wy", "wc", "expert"),
    )
    rows = ("groups", "wy", "wc")
    in_specs = (
        P(rows, None, "expert"),
        P("groups"),
        P("groups", None),
        P("groups"),
        P("groups"),
        P(),
        P(None, None, GROUP),
        P(None, None, GROUP),
        P(None, WIDE, "expert"),
        P(rows, None, "expert", None),
        P("groups", None, None, GROUP),
    )
    out_specs = P(rows, "expert")
    return jax.shard_map(
        per_device, mesh=split, in_specs=in_specs, out_specs=out_specs, check_vma=False
    )
```

profile of v0, /device:TPU:0, one launch (start us, length us, event | category | flops | bytes accessed | tf_op | source)
XLA Modules:
  0.0 282.4 jit_solution(12810220067142073298)
XLA Ops:
  6.5 3.0 %collective-permute-start.1 = (bf16[1,128,1536]{2,1,0:T(8,128)(2,1)}, bf16[1,128,1536]{2,1,0:T(8,128)(2,1)S(1)}, u32[]{:S(2)}, u32[]{:S(2)}) collective-permute-start(bf16[1,128,1536]{2,1,0:T(8,128)(2,1)} %param.11), channel_id=1, source_target_pairs={{0,8},{8,0},{1,9},{9,1},{2,10},{10,2},{3,11},{11,3},{4,12},{12,4},... | collective-permute-start | bytes 1179656 | tf_op jit(solution)/shard_map/ppermute | solution.py:42
  9.5 9.3 %collective-permute-done.1 = bf16[1,128,1536]{2,1,0:T(8,128)(2,1)S(1)} collective-permute-done((bf16[1,128,1536]{2,1,0:T(8,128)(2,1)}, bf16[1,128,1536]{2,1,0:T(8,128)(2,1)S(1)}, u32[]{:S(2)}, u32[]{:S(2)}) %collective-permute-start.1) | collective-permute-done | bytes 393248 | tf_op jit(solution)/shard_map/ppermute | solution.py:42
  18.8 0.7 compare_and_fusion.2
  19.5 0.1 broadcast_bitcast_fusion
  19.6 0.1 dynamic-slice
  19.7 0.9 collective-permute-done.2
  20.6 2.4 pad_maximum_fusion.1
  22.9 2.1 gather_fusion
  25.0 1.2 dynamic-slice_select_fusion
  26.3 1.8 collective-permute-start.5
  28.1 18.2 %collective-permute-done.5 = bf16[2,2,1536,64]{2,3,1,0:T(8,128)(2,1)} collective-permute-done((bf16[2,2,1536,64]{2,3,1,0:T(8,128)(2,1)}, bf16[2,2,1536,64]{2,3,1,0:T(8,128)(2,1)}, u32[]{:S(2)}, u32[]{:S(2)}) %collective-permute-start.5) | collective-permute-done | bytes 786464 | tf_op jit(solution)/shard_map/ppermute | solution.py:60
  46.3 0.6 gather_fusion.2
  47.0 1.9 collective-permute-done.6
  48.9 3.2 %pad_maximum_fusion = bf16[4,2,2,1536,64]{3,4,2,1,0:T(8,128)(2,1)} fusion(bf16[1,2,2,1536,64]{3,4,2,1,0:T(8,128)(2,1)} %bitcast.9, bf16[1,2,2,1536,64]{3,4,2,1,0:T(8,128)(2,1)} %bitcast.8, bf16[1,2,2,1536,64]{3,4,2,1,0:T(8,128)(2,1)} %bitcast.7, bf16[1,2,2,1536,64]{3,4,2,1,0:T(8,128)(2,1)} %bitcast.119), kind=kLoop, calls=%fused_computation.23 | loop fusion | flops 4718592 | bytes 6291456 | tf_op jit(solution)/shard_map/stack | solution.py:63
  52.1 2.5 gather_fusion.3
  54.6 23.7 %all-gather.5.cloned.1.call-done = bf16[192,6144]{1,0:T(8,128)(2,1)} async-done(((bf16[192,1536]{1,0:T(8,128)(2,1)}), bf16[192,6144]{1,0:T(8,128)(2,1)}) %all-gather.5.cloned.1.call-update) | async-done | bytes 2359312 | tf_op jit(solution)/shard_map/all_gather | solution.py:83
  78.3 0.2 broadcast_select_fusion
  78.5 1.1 copy-done.9
  79.6 0.5 fusion.33
  80.1 0.1 copy.18
  80.3 0.2 fusion.44
  80.5 15.9 %all-gather = bf16[192,1024]{0,1:T(8,128)(2,1)S(1)} all-gather(bf16[192,256]{0,1:T(8,128)(2,1)S(1)} %fusion.44), channel_id=2, replica_groups=mesh['groups'=2,'wy'=2,'wc'=2,'expert'=4] {'expert'}, dimensions={1}, use_global_device_ids=true | all-gather | bytes 491520 | tf_op jit(solution)/shard_map/all_gather | solution.py:88
  96.4 0.1 bitcast_convert_fusion
  96.6 0.1 collective-permute-start.7
  96.7 0.6 gather_fusion.1
  97.3 0.6 collective-permute-done.7
  97.9 0.1 maximum_select_fusion.1
  98.1 0.6 convolution_bitcast_fusion
  98.7 0.2 copy.20
  99.0 2.5 copy-done.10
  101.5 4.0 %maximum_select_fusion = bf16[384,6144]{1,0:T(8,128)(2,1)S(1)} fusion(bf16[192,6144]{1,0:T(8,128)(2,1)} %collective-permute-done.3, bf16[192,6144]{1,0:T(8,128)(2,1)S(1)} %copy-done.10, pred[]{:T(512)S(6)} %eq.14), kind=kLoop, calls=%fused_computation.22 | loop fusion | flops 21233664 | bytes 9437185 | tf_op jit(solution)/shard_map/jit(_where)/select_n | solution.py:93
  105.5 1.3 fusion.53
  107.0 8.1 %fusion.4 = f32[384,1024]{1,0:T(8,128)S(1)} fusion(bf16[384,6144]{1,0:T(8,128)(2,1)S(1)} %maximum_select_fusion, bf16[2,6144,1024]{2,1,0:T(8,128)(2,1)} %param.17), kind=kOutput, calls=%fused_computation.8 | convolution fusion | flops 4831838208 | bytes 18874368 | tf_op jit(solution)/shard_map/dot_general | solution.py:117
  115.1 9.0 %fusion.24 = bf16[384,1024]{1,0:T(8,128)(2,1)} fusion(f32[384,2,1024]{2,0,1:T(8,128)S(1)} %bitcast.114, f32[384,1024]{1,0:T(8,128)S(1)} %fusion.4, bf16[384,6144]{1,0:T(8,128)(2,1)S(1)} %maximum_select_fusion, bf16[2,6144,1024]{2,1,0:T(8,128)(2,1)} %param.18, f32[384]{0:T(512)S(1)} %get-tuple-element.8), kind=kOutput, calls=%fused_computation.30 | convolution fusion | flops 4835377152 | bytes 21235200 | tf_op jit(solution)/shard_map/dot_general | solution.py:121
  124.1 0.2 all-gather.7.cloned.1.call-start
  124.4 11.1 %fusion.10 = f32[384,1024]{1,0:T(8,128)S(1)} fusion(bf16[384,6144]{1,0:T(8,128)(2,1)} %copy-done.3, bf16[2,6144,1024]{2,1,0:T(8,128)(2,1)} %param.17), kind=kOutput, calls=%fused_computation.14 | convolution fusion | flops 4831838208 | bytes 18874368 | tf_op jit(solution)/shard_map/dot_general | solution.py:117
  135.5 9.1 %fusion.28 = bf16[384,1024]{1,0:T(8,128)(2,1)} fusion(f32[384,2,1024]{2,0,1:T(8,128)S(1)} %bitcast.115, f32[384,1024]{1,0:T(8,128)S(1)} %fusion.10, bf16[384,6144]{1,0:T(8,128)(2,1)S(1)} %copy-done.4, bf16[2,6144,1024]{2,1,0:T(8,128)(2,1)} %param.18, f32[384]{0:T(512)S(1)} %get-tuple-element.7), kind=kOutput, calls=%fused_computation.35 | convolution fusion | flops 4835377152 | bytes 21235200 | tf_op jit(solution)/shard_map/dot_general | solution.py:121
  144.6 41.7 %all-gather.9.cloned.1.call-done = bf16[384,4096]{1,0:T(8,128)(2,1)} async-done(((bf16[384,1024]{1,0:T(8,128)(2,1)}), bf16[384,4096]{1,0:T(8,128)(2,1)}) %all-gather.9.cloned.1.call-update) | async-done | bytes 3145744 | tf_op jit(solution)/shard_map/all_gather | solution.py:127
  186.3 10.0 %fusion = f32[384,1536]{1,0:T(8,128)} fusion(bf16[384,4096]{1,0:T(8,128)(2,1)} %all-gather.9.cloned.1.call-done, bf16[2,4096,1536]{2,1,0:T(8,128)(2,1)} %param.19), kind=kOutput, calls=%fused_computation.4 | convolution fusion | flops 4831838208 | bytes 18087936 | tf_op jit(solution)/shard_map/dot_general | solution.py:128
  196.4 53.7 %all-gather.7.cloned.1.call-done = bf16[384,4096]{1,0:T(8,128)(2,1)} async-done(((bf16[384,1024]{1,0:T(8,128)(2,1)}), bf16[384,4096]{1,0:T(8,128)(2,1)}) %all-gather.7.cloned.1.call-update) | async-done | bytes 3145744 | tf_op jit(solution)/shard_map/all_gather | solution.py:127
  250.1 9.3 %fusion.18 = f32[384,1536]{1,0:T(8,128)S(1)} fusion(f32[384,1536]{1,0:T(8,128)} %fusion, bf16[384,4096]{1,0:T(8,128)(2,1)} %all-gather.7.cloned.1.call-done, bf16[2,4096,1536]{2,1,0:T(8,128)(2,1)} %param.19), kind=kOutput, calls=%fused_computation.24 | convolution fusion | flops 4832428032 | bytes 20447232 | tf_op jit(solution)/shard_map/dot_general | solution.py:128
  259.4 1.4 copy-done.5
  260.8 0.1 select_bitcast_fusion
  261.0 2.8 %collective-permute-done.8 = f32[2,96,1536]{2,1,0:T(8,128)S(1)} collective-permute-done((f32[2,96,1536]{2,1,0:T(8,128)S(1)}, f32[2,96,1536]{2,1,0:T(8,128)S(1)}, u32[]{:S(2)}, u32[]{:S(2)}) %collective-permute-start.8) | collective-permute-done | bytes 1179680 | tf_op jit(solution)/shard_map/ppermute | solution.py:139
  263.8 2.0 bitcast_add_fusion
  265.9 1.5 collective-permute-start.9
  267.5 7.6 %collective-permute-done.9 = bf16[96,1536]{1,0:T(8,128)(2,1)S(1)} collective-permute-done((bf16[96,1536]{1,0:T(8,128)(2,1)S(1)}, bf16[96,1536]{1,0:T(8,128)(2,1)S(1)}, u32[]{:S(2)}, u32[]{:S(2)}) %collective-permute-start.9) | collective-permute-done | bytes 294944 | tf_op jit(solution)/shard_map/ppermute | solution.py:144
  275.1 0.8 fusion.38
  (53 shorter events, 0.6 us)
Async XLA Ops:
  6.5 90.2 %copy-start = (bf16[8,2,64,1024]{3,2,1,0:T(8,128)(2,1)S(1)}, bf16[8,2,64,1024]{3,2,1,0:T(8,128)(2,1)}, u32[]{:S(2)}) copy-start(bf16[8,2,64,1024]{3,2,1,0:T(8,128)(2,1)} %param.21) | copy-start | bytes 6291460
  6.5 71.8 %all-gather.5.cloned.1.call-start = ((), (), s32[]{:S(2)}) async-start(), calls=%async_computation | async-start | bytes 2949120 | tf_op jit(solution)/shard_map/all_gather | solution.py:83
  6.5 12.3 %collective-permute-start.1 = (bf16[1,128,1536]{2,1,0:T(8,128)(2,1)}, bf16[1,128,1536]{2,1,0:T(8,128)(2,1)S(1)}, u32[]{:S(2)}, u32[]{:S(2)}) collective-permute-start(bf16[1,128,1536]{2,1,0:T(8,128)(2,1)} %param.11), channel_id=1, source_target_pairs={{0,8},{8,0},{1,9},{9,1},{2,10},{10,2},{3,11},{11,3},{4,12},{12,4},... | collective-permute-start | bytes 1179656 | tf_op jit(solution)/shard_map/ppermute | solution.py:42
  9.5 10.2 %collective-permute-start = (bf16[1,128,1536]{2,1,0:T(8,128)(2,1)}, bf16[1,128,1536]{2,1,0:T(8,128)(2,1)S(1)}, u32[]{:S(2)}, u32[]{:S(2)}) collective-permute-start(bf16[1,128,1536]{2,1,0:T(8,128)(2,1)} %param.11), channel_id=1, source_target_pairs={{0,4},{4,0},{1,5},{5,1},{2,6},{6,2},{3,7},{7,3},{8,12},{12,8},{9,1... | collective-permute-start | bytes 1179656 | tf_op jit(solution)/shard_map/ppermute | solution.py:43
  18.8 1.7 collective-permute-start.2
  22.9 23.3 %copy-start.13 = (s32[3]{0:T(128)S(1)}, s32[3]{0:T(128)}, u32[]{:S(2)}) copy-start(s32[3]{0:T(128)} %param.14) | copy-start | bytes 40
  22.9 23.3 %copy-start.2 = (s32[8]{0:T(128)S(1)}, s32[8]{0:T(128)}, u32[]{:S(2)}) copy-start(s32[8]{0:T(128)} %param.15) | copy-start | bytes 100
  25.0 27.1 %copy-start.8 = (bf16[3,128,1536]{2,1,0:T(8,128)(2,1)}, bf16[3,128,1536]{2,1,0:T(8,128)(2,1)S(1)}, u32[]{:S(2)}) copy-start(bf16[3,128,1536]{2,1,0:T(8,128)(2,1)S(1)} %gather_fusion) | copy-start | bytes 3538948
  26.2 160.1 %all-gather.9.cloned.1.call-start = ((), (), s32[]{:S(2)}) async-start(), calls=%async_computation.2 | async-start | bytes 3932160 | tf_op jit(solution)/shard_map/all_gather | solution.py:127
  26.3 20.0 %collective-permute-start.5 = (bf16[2,2,1536,64]{2,3,1,0:T(8,128)(2,1)}, bf16[2,2,1536,64]{2,3,1,0:T(8,128)(2,1)}, u32[]{:S(2)}, u32[]{:S(2)}) collective-permute-start(bf16[2,2,1536,64]{2,3,1,0:T(8,128)(2,1)} %param.20), channel_id=1, source_target_pairs={{0,8},{8,0},{1,9},{9,1},{2,10},{10,2},{3,11},{11,3},{4,12},{12,4},... | collective-permute-start | bytes 2359304 | tf_op jit(solution)/shard_map/ppermute | solution.py:60
  28.1 18.9 %collective-permute-start.4 = (bf16[2,2,1536,64]{2,3,1,0:T(8,128)(2,1)}, bf16[2,2,1536,64]{2,3,1,0:T(8,128)(2,1)}, u32[]{:S(2)}, u32[]{:S(2)}) collective-permute-start(bf16[2,2,1536,64]{2,3,1,0:T(8,128)(2,1)} %param.20), channel_id=1, source_target_pairs={{0,4},{4,0},{1,5},{5,1},{2,6},{6,2},{3,7},{7,3},{8,12},{12,8},{9,1... | collective-permute-start | bytes 2359304 | tf_op jit(solution)/shard_map/ppermute | solution.py:61
  46.2 2.6 collective-permute-start.6
  78.3 1.3 copy-start.9
  78.3 20.7 %collective-permute-start.3 = (bf16[192,6144]{1,0:T(8,128)(2,1)}, bf16[192,6144]{1,0:T(8,128)(2,1)}, u32[]{:S(2)}, u32[]{:S(2)}) collective-permute-start(bf16[192,6144]{1,0:T(8,128)(2,1)} %all-gather.5.cloned.1.call-done), channel_id=1, source_target_pairs={{0,4},{4,0},{1,5},{5,1},{2,6},{6,2},{3,7},{7,3},{8,12},{12,8},{9,1... | collective-permute-start | bytes 7077896 | tf_op jit(solution)/shard_map/ppermute | solution.py:91
  80.1 16.6 %copy-start.12 = (s32[384,2]{0,1:T(2,128)S(1)}, s32[384,2]{0,1:T(2,128)}, u32[]{:S(2)}) copy-start(s32[384,2]{0,1:T(2,128)} %param.13) | copy-start | bytes 9220
  96.6 1.3 collective-permute-start.7
  98.7 2.8 copy-start.10
  98.9 16.2 %copy-start.6 = (f32[3,128,2,1024]{3,1,0,2:T(8,128)}, f32[3,128,2,1024]{3,1,0,2:T(8,128)S(1)}, u32[]{:S(2)}) copy-start(f32[3,128,2,1024]{3,1,0,2:T(8,128)S(1)} %copy.20) | copy-start | bytes 9437188
  98.9 6.6 %copy-start.11 = (bf16[6144,8]{0,1:T(8,128)(2,1)S(1)}, bf16[6144,8]{0,1:T(8,128)(2,1)}, u32[]{:S(2)}) copy-start(bf16[6144,8]{0,1:T(8,128)(2,1)} %param.16) | copy-start | bytes 294916
  105.5 9.6 %copy-start.3 = (bf16[384,6144]{1,0:T(8,128)(2,1)}, bf16[384,6144]{1,0:T(8,128)(2,1)S(1)}, u32[]{:S(2)}) copy-start(bf16[384,6144]{1,0:T(8,128)(2,1)S(1)} %maximum_select_fusion) | copy-start | bytes 14155780
  124.1 125.9 %all-gather.7.cloned.1.call-start = ((), (), s32[]{:S(2)}) async-start(), calls=%async_computation.1 | async-start | bytes 3932160 | tf_op jit(solution)/shard_map/all_gather | solution.py:127
  124.4 11.1 %copy-start.4 = (bf16[384,6144]{1,0:T(8,128)(2,1)S(1)}, bf16[384,6144]{1,0:T(8,128)(2,1)}, u32[]{:S(2)}) copy-start(bf16[384,6144]{1,0:T(8,128)(2,1)} %copy-done.3) | copy-start | bytes 14155780
  124.4 11.1 %copy-start.7 = (f32[3,128,2,1024]{3,1,0,2:T(8,128)S(1)}, f32[3,128,2,1024]{3,1,0,2:T(8,128)}, u32[]{:S(2)}) copy-start(f32[3,128,2,1024]{3,1,0,2:T(8,128)} %copy-done.6) | copy-start | bytes 9437188
  259.4 1.4 copy-start.5
  260.9 2.9 %collective-permute-start.8 = (f32[2,96,1536]{2,1,0:T(8,128)S(1)}, f32[2,96,1536]{2,1,0:T(8,128)S(1)}, u32[]{:S(2)}, u32[]{:S(2)}) collective-permute-start(f32[2,96,1536]{2,1,0:T(8,128)S(1)} %select_bitcast_fusion), channel_id=1, source_target_pairs={{0,4},{4,0},{1,5},{5,1},{2,6},{6,2},{3,7},{7,3},{8,12},{12,8},{9,1... | collective-permute-start | bytes 3538952 | tf_op jit(solution)/shard_map/ppermute | solution.py:139
  263.8 12.0 %copy-start.1 = (bf16[8,2,64,1024]{3,2,1,0:T(8,128)(2,1)S(1)}, bf16[8,2,64,1024]{3,2,1,0:T(8,128)(2,1)}, u32[]{:S(2)}) copy-start(bf16[8,2,64,1024]{3,2,1,0:T(8,128)(2,1)} %param.21) | copy-start | bytes 6291460
  265.9 9.1 %collective-permute-start.9 = (bf16[96,1536]{1,0:T(8,128)(2,1)S(1)}, bf16[96,1536]{1,0:T(8,128)(2,1)S(1)}, u32[]{:S(2)}, u32[]{:S(2)}) collective-permute-start(bf16[96,1536]{1,0:T(8,128)(2,1)S(1)} %fusion.42), channel_id=1, source_target_pairs={{0,8},{8,0},{1,9},{9,1},{2,10},{10,2},{3,11},{11,3},{4,12},{12,4},... | collective-permute-start | bytes 884744 | tf_op jit(solution)/shard_map/ppermute | solution.py:144
Sparse Core Ops, SparseCore 0:
  26.3 51.9 all-gather.4
  124.3 62.0 all-gather.8
  187.9 62.1 all-gather.6
where the time goes:
time: 283 us; the launch traced here: 282 us
  waiting for transfers between devices  160 us (57%)
  matrix products  59.1 us (21%)
  blocking collectives  15.9 us (6%)
  other arithmetic  15.3 us (5%)
  between operations  13.5 us (5%)
  local copies, waits for them, and re-layouts  11.5 us (4%)
  starting transfers between devices  6.73 us (2%)
    all_gather x2, waiting for transfers between devices, per_device(): gathered = lax.all_gather(hidden, 'expert', axis=1, tiled=True)  95.4 us
    all_gather x1, waiting for transfers between devices, per_device(): mine = lax.all_gather(mine_q, 'expert', axis=1, tiled=True)  23.7 us
    dot_general x2, matrix products, per_device(): jnp.dot(gathered, down_weight[expert_number], preferred_element_type=jnp....  19.3 us
    dot_general x2, matrix products, per_device(): jnp.dot(input_rows, gate_weight[expert_number], preferred_element_type=jn...  19.2 us
    ppermute x1, waiting for transfers between devices, per_device(): from_chip = lax.ppermute(adapter_down_weight, 'wy', swap)  18.2 us
    dot_general x2, matrix products, per_device(): jnp.dot(input_rows, up_weight[expert_number], preferred_element_type=jnp....  18.1 us
    all_gather x1, blocking collectives, per_device(): lax.all_gather(rank_q, 'expert', axis=1, tiled=False).astype(jnp.float32)  15.9 us
    ppermute x1, waiting for transfers between devices, per_device(): slot_chip = lax.ppermute(prompts, 'wy', pair)  9.32 us
  transfers between devices with their start and end apart: 13, of which 10 were waited for; matrix products, arithmetic and copies ran while one was open for 14% of the time, Pallas kernels for 0%

commit v1 on v0

--- a/solution.py
+++ b/solution.py
@@ -124,7 +124,16 @@
         hidden = (weight[:, expert_number, None] * jax.nn.silu(gate_pre) * up_value).astype(
             jnp.bfloat16
         )
-        gathered = lax.all_gather(hidden, "expert", axis=1, tiled=True)
+        ring = [hidden]
+        for hop in range(3):
+            ring.append(
+                lax.ppermute(ring[-1], "expert", [(dev, (dev + 1) % 4) for dev in range(4)])
+            )
+        gathered = jnp.roll(
+            jnp.concatenate(ring[::-1], axis=1),
+            (lax.axis_index("expert") + 1) * ring[0].shape[1],
+            axis=1,
+        )
         part = jnp.dot(gathered, down_weight[expert_number], preferred_element_type=jnp.float32)
         running = part if running is None else running + part
     return reduce_rows(running, core, cores).astype(jnp.bfloat16)

time: 283 us -> 274 us (0.968)
  waiting for transfers between devices: 160 us -> 148 us
    all_gather x2 -> x0, waiting for transfers between devices: 95.4 us -> none  [per_device(): gathered = lax.all_gather(hidden, 'expert', axis=1, tiled=True)]
    ppermute x0 -> x6, waiting for transfers between devices: none -> 83.2 us  [per_device(): lax.ppermute(ring[-1], 'expert', [(dev, (dev + 1) % 4) for dev in range(4)])]
    dot_general x2, matrix products: 19.3 us -> 25.4 us  [per_device(): jnp.dot(gathered, down_weight[expert_number], preferred_element_type=jnp....]
    dot_general x2, matrix products: 19.2 us -> 16.1 us  [per_device(): jnp.dot(input_rows, gate_weight[expert_number], preferred_element_type=jn...]
  transfers between devices with their start and end apart: 13 -> 17, of which waited for: 10 -> 14; matrix products, arithmetic and copies ran while one was open for 14% -> 12% of each run, Pallas kernels for 0% -> 0%
where the time goes in v1:
time: 274 us; the launch traced here: 273 us
  waiting for transfers between devices  148 us (54%)
  matrix products  61.8 us (23%)
  other arithmetic  16.2 us (6%)
  blocking collectives  16.2 us (6%)
  between operations  13.7 us (5%)
  local copies, waits for them, and re-layouts  9.22 us (3%)
  starting transfers between devices  7.79 us (3%)
    ppermute x6, waiting for transfers between devices, per_device(): lax.ppermute(ring[-1], 'expert', [(dev, (dev + 1) % 4) for dev in range(4)])  83.2 us
    dot_general x2, matrix products, per_device(): jnp.dot(gathered, down_weight[expert_number], preferred_element_type=jnp....  25.4 us
    all_gather x1, waiting for transfers between devices, per_device(): mine = lax.all_gather(mine_q, 'expert', axis=1, tiled=True)  23.7 us
    ppermute x1, waiting for transfers between devices, per_device(): from_chip = lax.ppermute(adapter_down_weight, 'wy', swap)  18.2 us
    dot_general x2, matrix products, per_device(): jnp.dot(input_rows, up_weight[expert_number], preferred_element_type=jnp....  16.5 us
    all_gather x1, blocking collectives, per_device(): lax.all_gather(rank_q, 'expert', axis=1, tiled=False).astype(jnp.float32)  16.2 us
    dot_general x2, matrix products, per_device(): jnp.dot(input_rows, gate_weight[expert_number], preferred_element_type=jn...  16.1 us
    ppermute x1, waiting for transfers between devices, per_device(): slot_chip = lax.ppermute(prompts, 'wy', pair)  9.32 us
  transfers between devices with their start and end apart: 17, of which 14 were waited for; matrix products, arithmetic and copies ran while one was open for 12% of the time, Pallas kernels for 0%

profile of v1, /device:TPU:0, one launch (start us, length us, event | category | flops | bytes accessed | tf_op | source)
XLA Modules:
  0.0 273.3 jit_solution(14417550357303377456)
XLA Ops:
  6.5 3.0 %collective-permute-start.1 = (bf16[1,128,1536]{2,1,0:T(8,128)(2,1)}, bf16[1,128,1536]{2,1,0:T(8,128)(2,1)S(1)}, u32[]{:S(2)}, u32[]{:S(2)}) collective-permute-start(bf16[1,128,1536]{2,1,0:T(8,128)(2,1)} %param.13), channel_id=1, source_target_pairs={{0,8},{8,0},{1,9},{9,1},{2,10},{10,2},{3,11},{11,3},{4,12},{12,4},... | collective-permute-start | bytes 1179656 | tf_op jit(solution)/shard_map/ppermute | solution.py:42
  9.5 9.3 %collective-permute-done.1 = bf16[1,128,1536]{2,1,0:T(8,128)(2,1)S(1)} collective-permute-done((bf16[1,128,1536]{2,1,0:T(8,128)(2,1)}, bf16[1,128,1536]{2,1,0:T(8,128)(2,1)S(1)}, u32[]{:S(2)}, u32[]{:S(2)}) %collective-permute-start.1) | collective-permute-done | bytes 393248 | tf_op jit(solution)/shard_map/ppermute | solution.py:42
  18.8 0.7 compare_and_fusion.2
  19.7 0.9 collective-permute-done.2
  20.6 2.4 pad_maximum_fusion.1
  22.9 2.0 gather_fusion
  25.0 1.1 dynamic-slice_select_fusion
  26.1 1.8 collective-permute-start.5
  27.9 18.2 %collective-permute-done.5 = bf16[2,2,1536,64]{2,3,1,0:T(8,128)(2,1)} collective-permute-done((bf16[2,2,1536,64]{2,3,1,0:T(8,128)(2,1)}, bf16[2,2,1536,64]{2,3,1,0:T(8,128)(2,1)}, u32[]{:S(2)}, u32[]{:S(2)}) %collective-permute-start.5) | collective-permute-done | bytes 786464 | tf_op jit(solution)/shard_map/ppermute | solution.py:60
  46.1 0.6 gather_fusion.2
  46.8 1.9 collective-permute-done.6
  48.7 3.2 %pad_maximum_fusion = bf16[4,2,2,1536,64]{3,4,2,1,0:T(8,128)(2,1)} fusion(bf16[1,2,2,1536,64]{3,4,2,1,0:T(8,128)(2,1)} %bitcast.9, bf16[1,2,2,1536,64]{3,4,2,1,0:T(8,128)(2,1)} %bitcast.8, bf16[1,2,2,1536,64]{3,4,2,1,0:T(8,128)(2,1)} %bitcast.7, bf16[1,2,2,1536,64]{3,4,2,1,0:T(8,128)(2,1)} %bitcast.117), kind=kLoop, calls=%fused_computation.53 | loop fusion | flops 4718592 | bytes 6291456 | tf_op jit(solution)/shard_map/stack | solution.py:63
  52.0 2.5 gather_fusion.3
  54.5 23.7 %all-gather.3.cloned.1.call-done = bf16[192,6144]{1,0:T(8,128)(2,1)} async-done(((bf16[192,1536]{1,0:T(8,128)(2,1)}), bf16[192,6144]{1,0:T(8,128)(2,1)}) %all-gather.3.cloned.1.call-update) | async-done | bytes 2359312 | tf_op jit(solution)/shard_map/all_gather | solution.py:83
  78.2 0.2 broadcast_select_fusion
  78.4 1.8 fusion.53
  80.2 0.1 copy.18
  80.4 0.2 fusion.64
  80.6 16.2 %all-gather = bf16[192,1024]{0,1:T(8,128)(2,1)S(1)} all-gather(bf16[192,256]{0,1:T(8,128)(2,1)S(1)} %fusion.64), channel_id=2, replica_groups=mesh['groups'=2,'wy'=2,'wc'=2,'expert'=4] {'expert'}, dimensions={1}, use_global_device_ids=true | all-gather | bytes 491520 | tf_op jit(solution)/shard_map/all_gather | solution.py:88
  96.8 0.1 bitcast_convert_fusion
  97.1 0.6 gather_fusion.1
  97.7 0.6 collective-permute-done.7
  98.3 0.1 maximum_select_fusion.1
  98.4 0.6 convolution_bitcast_fusion
  99.1 0.2 copy.20
  99.3 1.4 copy-done.5
  100.7 4.0 %maximum_select_fusion = bf16[384,6144]{1,0:T(8,128)(2,1)S(1)} fusion(bf16[192,6144]{1,0:T(8,128)(2,1)} %collective-permute-done.3, bf16[192,6144]{1,0:T(8,128)(2,1)S(1)} %copy-done.5, pred[]{:T(512)S(6)} %eq.16), kind=kLoop, calls=%fused_computation.38 | loop fusion | flops 21233664 | bytes 9437185 | tf_op jit(solution)/shard_map/jit(_where)/select_n | solution.py:93
  104.8 8.1 %fusion.4 = f32[384,1024]{1,0:T(8,128)S(1)} fusion(bf16[384,6144]{1,0:T(8,128)(2,1)S(1)} %maximum_select_fusion, bf16[2,6144,1024]{2,1,0:T(8,128)(2,1)} %param.19), kind=kOutput, calls=%fused_computation.8 | convolution fusion | flops 4831838208 | bytes 18874368 | tf_op jit(solution)/shard_map/dot_general | solution.py:117
  112.9 8.0 %fusion.10 = f32[384,1024]{1,0:T(8,128)S(1)} fusion(bf16[384,6144]{1,0:T(8,128)(2,1)S(1)} %maximum_select_fusion, bf16[2,6144,1024]{2,1,0:T(8,128)(2,1)} %param.19), kind=kOutput, calls=%fused_computation.14 | convolution fusion | flops 4831838208 | bytes 18874368 | tf_op jit(solution)/shard_map/dot_general | solution.py:117
  120.9 1.3 fusion.77
  122.4 8.2 %fusion.44 = bf16[384,1024]{1,0:T(8,128)(2,1)S(1)} fusion(f32[384,2,1024]{2,0,1:T(8,128)S(1)} %bitcast.112, f32[384,1024]{1,0:T(8,128)S(1)} %fusion.4, bf16[384,6144]{1,0:T(8,128)(2,1)S(1)} %maximum_select_fusion, bf16[2,6144,1024]{2,1,0:T(8,128)(2,1)} %param.20, f32[384]{0:T(512)S(1)} %get-tuple-element.9), kind=kOutput, calls=%fused_computation.60 | convolution fusion | flops 4835377152 | bytes 21235200 | tf_op jit(solution)/shard_map/dot_general | solution.py:121
  130.6 8.3 %fusion.48 = bf16[384,1024]{1,0:T(8,128)(2,1)S(1)} fusion(f32[384,2,1024]{2,0,1:T(8,128)S(1)} %bitcast.113, f32[384,1024]{1,0:T(8,128)S(1)} %fusion.10, bf16[384,6144]{1,0:T(8,128)(2,1)S(1)} %maximum_select_fusion, bf16[2,6144,1024]{2,1,0:T(8,128)(2,1)} %param.20, f32[384]{0:T(512)S(1)} %get-tuple-element.8), kind=kOutput, calls=%fused_computation.65 | convolution fusion | flops 4835377152 | bytes 21235200 | tf_op jit(solution)/shard_map/dot_general | solution.py:121
  139.0 1.3 collective-permute-start.8
  140.3 12.5 %collective-permute-done.11 = bf16[384,1024]{1,0:T(8,128)(2,1)S(1)} collective-permute-done((bf16[384,1024]{1,0:T(8,128)(2,1)S(1)}, bf16[384,1024]{1,0:T(8,128)(2,1)S(1)}, u32[]{:S(2)}, u32[]{:S(2)}) %collective-permute-start.11) | collective-permute-done | bytes 786464 | tf_op jit(solution)/shard_map/ppermute | solution.py:130
  152.8 17.0 %collective-permute-done.8 = bf16[384,1024]{1,0:T(8,128)(2,1)} collective-permute-done((bf16[384,1024]{1,0:T(8,128)(2,1)S(1)}, bf16[384,1024]{1,0:T(8,128)(2,1)}, u32[]{:S(2)}, u32[]{:S(2)}) %collective-permute-start.8) | collective-permute-done | bytes 786464 | tf_op jit(solution)/shard_map/ppermute | solution.py:130
  169.8 16.8 %collective-permute-done.12 = bf16[384,1024]{1,0:T(8,128)(2,1)} collective-permute-done((bf16[384,1024]{1,0:T(8,128)(2,1)S(1)}, bf16[384,1024]{1,0:T(8,128)(2,1)}, u32[]{:S(2)}, u32[]{:S(2)}) %collective-permute-start.12) | collective-permute-done | bytes 786464 | tf_op jit(solution)/shard_map/ppermute | solution.py:130
  186.6 16.8 %collective-permute-done.9 = bf16[384,1024]{1,0:T(8,128)(2,1)} collective-permute-done((bf16[384,1024]{1,0:T(8,128)(2,1)}, bf16[384,1024]{1,0:T(8,128)(2,1)}, u32[]{:S(2)}, u32[]{:S(2)}) %collective-permute-start.9) | collective-permute-done | bytes 786464 | tf_op jit(solution)/shard_map/ppermute | solution.py:130
  203.5 16.8 %collective-permute-done.13 = bf16[384,1024]{1,0:T(8,128)(2,1)} collective-permute-done((bf16[384,1024]{1,0:T(8,128)(2,1)}, bf16[384,1024]{1,0:T(8,128)(2,1)}, u32[]{:S(2)}, u32[]{:S(2)}) %collective-permute-start.13) | collective-permute-done | bytes 786464 | tf_op jit(solution)/shard_map/ppermute | solution.py:130
  220.3 12.8 %fusion = f32[384,1536]{1,0:T(8,128)S(1)} fusion(bf16[2,4096,1536]{2,1,0:T(8,128)(2,1)} %param.21, s32[]{:T(128)S(6)} %select_n.163, bf16[384,1024]{1,0:T(8,128)(2,1)} %collective-permute-done.13, bf16[384,1024]{1,0:T(8,128)(2,1)} %collective-permute-done.12, bf16[384,1024]{1,0:T(8,128)(2,1)S(1)} %collective-permute-done.11, bf16[384,1024]{1,0:T(8,128)(2,1)S(1)} %fusion.44), kind=kOutput, calls=%fused_computation.4 | convolution fusion | flops 4857004032 | bytes 18087940 | tf_op jit(solution)/shard_map/dot_general | solution.py:137
  233.1 3.2 %collective-permute-done.10 = bf16[384,1024]{1,0:T(8,128)(2,1)S(1)} collective-permute-done((bf16[384,1024]{1,0:T(8,128)(2,1)}, bf16[384,1024]{1,0:T(8,128)(2,1)S(1)}, u32[]{:S(2)}, u32[]{:S(2)}) %collective-permute-start.10) | collective-permute-done | bytes 786464 | tf_op jit(solution)/shard_map/ppermute | solution.py:130
  236.3 12.6 %fusion.36 = f32[384,1536]{1,0:T(8,128)S(1)} fusion(f32[384,1536]{1,0:T(8,128)S(1)} %fusion, bf16[2,4096,1536]{2,1,0:T(8,128)(2,1)} %param.21, s32[]{:T(128)S(6)} %select_n.163, bf16[384,1024]{1,0:T(8,128)(2,1)S(1)} %collective-permute-done.10, bf16[384,1024]{1,0:T(8,128)(2,1)} %collective-permute-done.9, bf16[384,1024]{1,0:T(8,128)(2,1)} %collective-permute-done.8, ...), kind=kOutput, calls=%fused_computation.54 | convolution fusion | flops 4857593856 | bytes 20447236 | tf_op jit(solution)/shard_map/dot_general | solution.py:137
  248.9 1.4 copy-done.3
  250.4 1.2 select_bitcast_fusion
  251.5 3.1 %collective-permute-done.14 = f32[2,96,1536]{2,1,0:T(8,128)S(1)} collective-permute-done((f32[2,96,1536]{2,1,0:T(8,128)}, f32[2,96,1536]{2,1,0:T(8,128)S(1)}, u32[]{:S(2)}, u32[]{:S(2)}) %collective-permute-start.14) | collective-permute-done | bytes 1179680 | tf_op jit(solution)/shard_map/ppermute | solution.py:148
  254.6 1.9 bitcast_add_fusion
  256.5 1.5 collective-permute-start.15
  258.0 7.6 %collective-permute-done.15 = bf16[96,1536]{1,0:T(8,128)(2,1)S(1)} collective-permute-done((bf16[96,1536]{1,0:T(8,128)(2,1)S(1)}, bf16[96,1536]{1,0:T(8,128)(2,1)S(1)}, u32[]{:S(2)}, u32[]{:S(2)}) %collective-permute-start.15) | collective-permute-done | bytes 294944 | tf_op jit(solution)/shard_map/ppermute | solution.py:153
  265.6 0.8 fusion.58
  (49 shorter events, 0.7 us)
Async XLA Ops:
  6.5 90.5 %copy-start = (bf16[8,2,64,1024]{3,2,1,0:T(8,128)(2,1)S(1)}, bf16[8,2,64,1024]{3,2,1,0:T(8,128)(2,1)}, u32[]{:S(2)}) copy-start(bf16[8,2,64,1024]{3,2,1,0:T(8,128)(2,1)} %param.23) | copy-start | bytes 6291460
  6.5 71.7 %all-gather.3.cloned.1.call-start = ((), (), s32[]{:S(2)}) async-start(), calls=%async_computation | async-start | bytes 2949120 | tf_op jit(solution)/shard_map/all_gather | solution.py:83
  6.5 12.3 %collective-permute-start.1 = (bf16[1,128,1536]{2,1,0:T(8,128)(2,1)}, bf16[1,128,1536]{2,1,0:T(8,128)(2,1)S(1)}, u32[]{:S(2)}, u32[]{:S(2)}) collective-permute-start(bf16[1,128,1536]{2,1,0:T(8,128)(2,1)} %param.13), channel_id=1, source_target_pairs={{0,8},{8,0},{1,9},{9,1},{2,10},{10,2},{3,11},{11,3},{4,12},{12,4},... | collective-permute-start | bytes 1179656 | tf_op jit(solution)/shard_map/ppermute | solution.py:42
  9.5 10.2 %collective-permute-start = (bf16[1,128,1536]{2,1,0:T(8,128)(2,1)}, bf16[1,128,1536]{2,1,0:T(8,128)(2,1)S(1)}, u32[]{:S(2)}, u32[]{:S(2)}) collective-permute-start(bf16[1,128,1536]{2,1,0:T(8,128)(2,1)} %param.13), channel_id=1, source_target_pairs={{0,4},{4,0},{1,5},{5,1},{2,6},{6,2},{3,7},{7,3},{8,12},{12,8},{9,1... | collective-permute-start | bytes 1179656 | tf_op jit(solution)/shard_map/ppermute | solution.py:43
  18.8 1.7 collective-permute-start.2
  19.7 26.4 %copy-start.8 = (s32[3]{0:T(128)S(1)}, s32[3]{0:T(128)}, u32[]{:S(2)}) copy-start(s32[3]{0:T(128)} %param.16) | copy-start | bytes 40
  19.7 26.5 %copy-start.2 = (s32[8]{0:T(128)S(1)}, s32[8]{0:T(128)}, u32[]{:S(2)}) copy-start(s32[8]{0:T(128)} %param.17) | copy-start | bytes 100
  24.9 27.0 %copy-start.4 = (bf16[3,128,1536]{2,1,0:T(8,128)(2,1)}, bf16[3,128,1536]{2,1,0:T(8,128)(2,1)S(1)}, u32[]{:S(2)}) copy-start(bf16[3,128,1536]{2,1,0:T(8,128)(2,1)S(1)} %gather_fusion) | copy-start | bytes 3538948
  26.1 20.0 %collective-permute-start.5 = (bf16[2,2,1536,64]{2,3,1,0:T(8,128)(2,1)}, bf16[2,2,1536,64]{2,3,1,0:T(8,128)(2,1)}, u32[]{:S(2)}, u32[]{:S(2)}) collective-permute-start(bf16[2,2,1536,64]{2,3,1,0:T(8,128)(2,1)} %param.22), channel_id=1, source_target_pairs={{0,8},{8,0},{1,9},{9,1},{2,10},{10,2},{3,11},{11,3},{4,12},{12,4},... | collective-permute-start | bytes 2359304 | tf_op jit(solution)/shard_map/ppermute | solution.py:60
  27.9 18.9 %collective-permute-start.4 = (bf16[2,2,1536,64]{2,3,1,0:T(8,128)(2,1)}, bf16[2,2,1536,64]{2,3,1,0:T(8,128)(2,1)}, u32[]{:S(2)}, u32[]{:S(2)}) collective-permute-start(bf16[2,2,1536,64]{2,3,1,0:T(8,128)(2,1)} %param.22), channel_id=1, source_target_pairs={{0,4},{4,0},{1,5},{5,1},{2,6},{6,2},{3,7},{7,3},{8,12},{12,8},{9,1... | collective-permute-start | bytes 2359304 | tf_op jit(solution)/shard_map/ppermute | solution.py:61
  46.1 2.6 collective-permute-start.6
  78.2 21.1 %collective-permute-start.3 = (bf16[192,6144]{1,0:T(8,128)(2,1)}, bf16[192,6144]{1,0:T(8,128)(2,1)}, u32[]{:S(2)}, u32[]{:S(2)}) collective-permute-start(bf16[192,6144]{1,0:T(8,128)(2,1)} %all-gather.3.cloned.1.call-done), channel_id=1, source_target_pairs={{0,4},{4,0},{1,5},{5,1},{2,6},{6,2},{3,7},{7,3},{8,12},{12,8},{9,1... | collective-permute-start | bytes 7077896 | tf_op jit(solution)/shard_map/ppermute | solution.py:91
  80.2 16.8 %copy-start.7 = (s32[384,2]{0,1:T(2,128)S(1)}, s32[384,2]{0,1:T(2,128)}, u32[]{:S(2)}) copy-start(s32[384,2]{0,1:T(2,128)} %param.15) | copy-start | bytes 9220
  97.0 1.3 collective-permute-start.7
  99.1 1.7 copy-start.5
  112.9 8.1 %copy-start.6 = (bf16[6144,8]{0,1:T(8,128)(2,1)S(1)}, bf16[6144,8]{0,1:T(8,128)(2,1)}, u32[]{:S(2)}) copy-start(bf16[6144,8]{0,1:T(8,128)(2,1)} %param.18) | copy-start | bytes 294916
  130.6 22.2 %collective-permute-start.11 = (bf16[384,1024]{1,0:T(8,128)(2,1)S(1)}, bf16[384,1024]{1,0:T(8,128)(2,1)S(1)}, u32[]{:S(2)}, u32[]{:S(2)}) collective-permute-start(bf16[384,1024]{1,0:T(8,128)(2,1)S(1)} %fusion.44), channel_id=1, source_target_pairs={{0,1},{1,2},{2,3},{3,0},{4,5},{5,6},{6,7},{7,4},{8,9},{9,10},{10,1... | collective-permute-start | bytes 2359304 | tf_op jit(solution)/shard_map/ppermute | solution.py:130
  139.0 30.8 %collective-permute-start.8 = (bf16[384,1024]{1,0:T(8,128)(2,1)S(1)}, bf16[384,1024]{1,0:T(8,128)(2,1)}, u32[]{:S(2)}, u32[]{:S(2)}) collective-permute-start(bf16[384,1024]{1,0:T(8,128)(2,1)S(1)} %fusion.48), channel_id=1, source_target_pairs={{0,1},{1,2},{2,3},{3,0},{4,5},{5,6},{6,7},{7,4},{8,9},{9,10},{10,1... | collective-permute-start | bytes 2359304 | tf_op jit(solution)/shard_map/ppermute | solution.py:130
  152.8 33.8 %collective-permute-start.12 = (bf16[384,1024]{1,0:T(8,128)(2,1)S(1)}, bf16[384,1024]{1,0:T(8,128)(2,1)}, u32[]{:S(2)}, u32[]{:S(2)}) collective-permute-start(bf16[384,1024]{1,0:T(8,128)(2,1)S(1)} %collective-permute-done.11), channel_id=1, source_target_pairs={{0,1},{1,2},{2,3},{3,0},{4,5},{5,6},{6,7},{7,4},{8,9},{9,10},{10,1... | collective-permute-start | bytes 2359304 | tf_op jit(solution)/shard_map/ppermute | solution.py:130
  169.8 33.7 %collective-permute-start.9 = (bf16[384,1024]{1,0:T(8,128)(2,1)}, bf16[384,1024]{1,0:T(8,128)(2,1)}, u32[]{:S(2)}, u32[]{:S(2)}) collective-permute-start(bf16[384,1024]{1,0:T(8,128)(2,1)} %collective-permute-done.8), channel_id=1, source_target_pairs={{0,1},{1,2},{2,3},{3,0},{4,5},{5,6},{6,7},{7,4},{8,9},{9,10},{10,1... | collective-permute-start | bytes 2359304 | tf_op jit(solution)/shard_map/ppermute | solution.py:130
  186.6 33.7 %collective-permute-start.13 = (bf16[384,1024]{1,0:T(8,128)(2,1)}, bf16[384,1024]{1,0:T(8,128)(2,1)}, u32[]{:S(2)}, u32[]{:S(2)}) collective-permute-start(bf16[384,1024]{1,0:T(8,128)(2,1)} %collective-permute-done.12), channel_id=1, source_target_pairs={{0,1},{1,2},{2,3},{3,0},{4,5},{5,6},{6,7},{7,4},{8,9},{9,10},{10,1... | collective-permute-start | bytes 2359304 | tf_op jit(solution)/shard_map/ppermute | solution.py:130
  203.5 32.8 %collective-permute-start.10 = (bf16[384,1024]{1,0:T(8,128)(2,1)}, bf16[384,1024]{1,0:T(8,128)(2,1)S(1)}, u32[]{:S(2)}, u32[]{:S(2)}) collective-permute-start(bf16[384,1024]{1,0:T(8,128)(2,1)} %collective-permute-done.9), channel_id=1, source_target_pairs={{0,1},{1,2},{2,3},{3,0},{4,5},{5,6},{6,7},{7,4},{8,9},{9,10},{10,1... | collective-permute-start | bytes 2359304 | tf_op jit(solution)/shard_map/ppermute | solution.py:130
  248.9 1.4 copy-start.3
  251.5 3.1 %collective-permute-start.14 = (f32[2,96,1536]{2,1,0:T(8,128)}, f32[2,96,1536]{2,1,0:T(8,128)S(1)}, u32[]{:S(2)}, u32[]{:S(2)}) collective-permute-start(f32[2,96,1536]{2,1,0:T(8,128)} %select_bitcast_fusion), channel_id=1, source_target_pairs={{0,4},{4,0},{1,5},{5,1},{2,6},{6,2},{3,7},{7,3},{8,12},{12,8},{9,1... | collective-permute-start | bytes 3538952 | tf_op jit(solution)/shard_map/ppermute | solution.py:148
  251.5 14.9 %copy-start.1 = (bf16[8,2,64,1024]{3,2,1,0:T(8,128)(2,1)S(1)}, bf16[8,2,64,1024]{3,2,1,0:T(8,128)(2,1)}, u32[]{:S(2)}) copy-start(bf16[8,2,64,1024]{3,2,1,0:T(8,128)(2,1)} %param.23) | copy-start | bytes 6291460
  256.5 9.1 %collective-permute-start.15 = (bf16[96,1536]{1,0:T(8,128)(2,1)S(1)}, bf16[96,1536]{1,0:T(8,128)(2,1)S(1)}, u32[]{:S(2)}, u32[]{:S(2)}) collective-permute-start(bf16[96,1536]{1,0:T(8,128)(2,1)S(1)} %fusion.62), channel_id=1, source_target_pairs={{0,8},{8,0},{1,9},{9,1},{2,10},{10,2},{3,11},{11,3},{4,12},{12,4},... | collective-permute-start | bytes 884744 | tf_op jit(solution)/shard_map/ppermute | solution.py:153
Sparse Core Ops, SparseCore 0:
  26.2 51.9 all-gather.2
